TPU v7x, 512 devices: a whole 4x4x16 slice. The times are simulated.
512 devices in a mesh: pipe: 16 (over z_hi, y), zero: 32 (over z_lo, x, core).
Axes of the slice: x: 4, y: 4, z: 16 (z_hi: 4, z_lo: 4; z = z_hi * 4 + z_lo), core: 2. Of those that a mesh axis runs over, the one named last changes fastest.
Arguments:
- residual: bfloat16 [16, 2048, 4096], P('pipe', 'zero'), may hold values from -6 to 6
- norm_gain: bfloat16 [16, 4096], P('pipe'), may hold values from 0.099609375 to 1.8984375
- queries: bfloat16 [16, 2048, 4096], P('pipe', 'zero'), may hold values from -74 to 74
- cached_kv: bfloat16 [16, 512, 1024], P('pipe', 'zero'), may hold values from -6 to 6
- panel_blocks: bfloat16 [16, 160, 128, 128], P('pipe', 'zero'), may hold values from -0.125 to 0.125
- block_rows: int32 [16, 8, 20], P('pipe'), may hold values from 0 to 31, as said below
- counts: int32 [16, 8], P('pipe'), may hold values from 12 to 20, as said below
Outputs:
- passed: bfloat16 [16, 2048, 4096], P('pipe', 'zero')
- new_kv: bfloat16 [16, 2048, 1024], P('pipe', 'zero')
Inputs may be any that keep to these rules, and one draw needn't show every extreme that they name: `block_rows`: row blocks named by the slots of one panel are all different. `counts`: slots at or beyond a panel's count are padding.
All inputs are finite; a program needn't handle non-finite values.
Results may differ from a plain program's by a relative error of at most 0.0047.
The roundings to bfloat16 on the way count: a program that leaves them out, or rounds other values in their place, can miss the bound.
Values may be sent and summed in bfloat16 or wider, within the bound.
No kernel may reach another device: no remote copies, remote signals or barrier semaphores. Data moves between devices by JAX's collectives and lax.ppermute only.
A program may use at most 64 MiB of HBM per device.

v0:
```python
import math
import jax
import jax.numpy as jnp
from jax import lax
from jax.sharding import PartitionSpec as P

QH = 32
KVH = 4
HD = 128


def passed_along(block, axis, distance):
    devices = range(lax.axis_size(axis))
    route = [((i - distance) % len(devices), i) for i in devices]
    return lax.ppermute(block, axis, route)


def local(residual, norm_gain, queries, cached_kv, panel_blocks, block_rows, counts):
    row_count = residual.shape[1]
    model_width = residual.shape[2]
    zero_index = lax.axis_index("zero")
    stream = residual[0].astype(jnp.float32)
    normed = (
        stream
        * lax.rsqrt(jnp.mean(stream * stream, axis=-1, keepdims=True) + 1e-05)
        * norm_gain[0].astype(jnp.float32)
    ).astype(jnp.bfloat16)
    block_size = panel_blocks.shape[-1]
    panels = block_rows.shape[1]
    slot_depth = block_rows.shape[2]
    row_table = block_rows[0].reshape(-1)
    slot_live = (
        (jnp.arange(slot_depth)[None, :] < counts[0][:, None]).astype(jnp.float32).reshape(-1)
    )
    normed_grid = normed.reshape(row_count, model_width // block_size, block_size)
    kv_heads = KVH
    head_size = HD
    group_size = QH // KVH
    kv_width = kv_heads * head_size
    score_scale = 1.0 / math.sqrt(head_size)
    query_grid = queries[0].reshape(row_count, kv_heads, group_size, head_size)
    first_query = zero_index * row_count
    query_pos = first_query + jnp.arange(row_count)
    initial = (
        jnp.full((kv_heads, row_count, group_size), -1e30, jnp.float32),
        jnp.zeros((kv_heads, row_count, group_size), jnp.float32),
        jnp.zeros((kv_heads, row_count, group_size, head_size), jnp.float32),
    )

    def absorb(running, portion, visible):
        run_max, run_sum, run_acc = running
        key_count = portion.shape[0]
        key_grid = portion[:, :kv_width].reshape(key_count, kv_heads, head_size)
        value_grid = portion[:, kv_width:].reshape(key_count, kv_heads, head_size)
        scores = (
            jnp.einsum("rgjd,ngd->grjn", query_grid, key_grid, preferred_element_type=jnp.float32)
            * score_scale
        )
        visible_mask = visible[None, :, None, :]
        new_max = jnp.maximum(run_max, jnp.max(jnp.where(visible_mask, scores, -1e30), axis=-1))
        shrink = jnp.exp(run_max - new_max)
        weights = jnp.where(visible_mask, jnp.exp(scores - new_max[..., None]), 0.0)
        new_sum = run_sum * shrink + jnp.sum(weights, axis=-1)
        new_acc = run_acc * shrink[..., None] + jnp.einsum(
            "grjn,ngd->grjd",
            weights.astype(jnp.bfloat16),
            value_grid,
            preferred_element_type=jnp.float32,
        )
        return (new_max, new_sum, new_acc)

    zero_size = lax.axis_size("zero")
    local_slots = panel_blocks.shape[1]
    weight_rows = local_slots * block_size
    cache_local = cached_kv[0].reshape(-1, block_size)
    packed = jnp.concatenate(
        [panel_blocks[0].reshape(weight_rows, block_size), cache_local], axis=0
    )
    gathered = lax.all_gather(packed, "zero", axis=0, tiled=True).reshape(
        zero_size, packed.shape[0], block_size
    )
    all_blocks = gathered[:, :weight_rows].reshape(zero_size * local_slots, block_size, block_size)
    cache_portion = gathered[:, weight_rows:].reshape(
        zero_size * cached_kv.shape[1], cached_kv.shape[2]
    )
    chosen = jnp.take(normed_grid, row_table, axis=1)
    slot_terms = jnp.einsum("rsk,skn->rsn", chosen, all_blocks, preferred_element_type=jnp.float32)
    slot_terms = slot_terms * slot_live[None, :, None]
    summed = slot_terms.reshape(row_count, panels, slot_depth, block_size).sum(axis=2)
    kv_new = summed.reshape(row_count, panels * block_size).astype(jnp.bfloat16)
    softmax_state = absorb(
        initial, cache_portion, jnp.ones((row_count, cache_portion.shape[0]), bool)
    )
    portion = lax.all_gather(kv_new, "zero", axis=0, tiled=True)
    key_pos = jnp.arange(portion.shape[0])
    visible = key_pos[None, :] <= query_pos[:, None]
    softmax_state = lax.cond(
        jnp.int32(0) <= first_query + row_count - 1,
        lambda state_in: absorb(state_in, portion, visible),
        lambda state_in: state_in,
        softmax_state,
    )
    run_max, denominator, run_acc = softmax_state
    attended = run_acc / denominator[..., None]
    attended = jnp.transpose(attended, (1, 0, 2, 3)).reshape(
        row_count, kv_heads * group_size * head_size
    )
    updated = (stream + attended).astype(jnp.bfloat16)
    passed = passed_along(updated[None], "pipe", 1)
    return (passed, kv_new[None])


def solution(mesh):
    in_specs = (
        P("pipe", "zero", None),
        P("pipe", None),
        P("pipe", "zero", None),
        P("pipe", "zero", None),
        P("pipe", "zero", None, None),
        P("pipe", None, None),
        P("pipe", None),
    )
    out_specs = (P("pipe", "zero", None), P("pipe", "zero", None))
    return jax.shard_map(local, mesh=mesh, in_specs=in_specs, out_specs=out_specs, check_vma=False)
```

profile of v0, /device:TPU:96, one launch (start us, length us, event | category | flops | bytes accessed | tf_op | source)
XLA Modules:
  0.0 260.9 jit_solution(13501119565918339690)
XLA Ops:
  7.2 0.0 all-gather.3.cloned.1.call-start
  7.2 0.8 reshape_squeeze.15
  8.1 1.6 pad_maximum_fusion
  9.7 0.0 all-gather.3.cloned.1.call-update
  9.7 0.0 all-gather.5.cloned.1.call-start
  9.8 0.8 reshape_squeeze.18
  10.5 0.8 reshape_squeeze.17
  11.3 1.1 convert_bitcast_fusion
  12.4 0.2 copy.84
  12.6 0.1 fusion.33
  12.7 0.1 reshape.143
  12.8 0.2 fusion.27
  13.0 0.7 fusion.30
  13.7 1.1 gather_fusion
  14.8 68.7 %all-gather.3.cloned.1.call-done = bf16[24576,128]{1,0:T(8,128)(2,1)} async-done(((bf16[768,128]{1,0:T(8,128)(2,1)}), bf16[24576,128]{1,0:T(8,128)(2,1)}) %all-gather.3.cloned.1.call-update) | async-done | bytes 6291472 | tf_op jit(solution)/shard_map/all_gather | solution.py:79
  83.5 2.8 %slice.29 = bf16[32,640,128]{2,1,0:T(8,128)(2,1)S(1)} slice(bf16[32,768,128]{2,1,0:T(8,128)(2,1)} %bitcast.70), slice={[0:32], [0:640], [0:128]} | slice | bytes 10485760 | tf_op jit(solution)/shard_map/slice | solution.py:82
  86.4 3.7 %broadcast_multiply_fusion = f32[160,128,64]{1,2,0:T(8,128)} fusion(f32[160]{0:T(256)S(1)} %reshape.143, bf16[160,128,128]{2,1,0:T(8,128)(2,1)S(1)} %bitcast.68, bf16[160,64,128]{2,1,0:T(8,128)(2,1)S(1)} %gather_fusion, pred[160]{0:T(512)(128)(4,1)S(1)} %compare_and_fusion), kind=kOutput, calls=%fused_computation.24 | convolution fusion | flops 338165760 | bytes 13108000 | tf_op jit(solution)/shard_map/rsk,skn->rsn/dot_general | solution.py:87
  90.1 3.0 %reduce_sum.38 = bf16[64,8,128]{2,0,1:T(8,128)(2,1)S(1)} reduce(f32[64,8,20,128]{3,0,2,1:T(8,128)} %bitcast.67, f32[]{:T(128)} %constant.28.clone.1), dimensions={2}, to_apply=%region_3.4 | reduce | flops 1245184 | bytes 5373956 | tf_op jit(solution)/shard_map/reduce_sum | solution.py:89
  93.1 0.7 copy_bitcast_fusion
  93.8 0.1 copy.83
  93.9 1.3 slice.26
  95.2 0.5 reshape.135
  95.7 0.1 fusion.37
  95.8 0.2 copy.54
  96.0 0.8 bitcast_reduce_fusion
  96.8 1.1 fusion.13
  97.9 0.1 copy.57
  98.0 1.0 copy.58
  99.0 3.4 %fusion.23 = f32[4,64,8,128]{3,2,1,0:T(8,128)} fusion(bf16[512,4,128,1]{0,2,3,1:T(8,128)(2,1)} %bitcast.78, bf16[4,64,8,512]{3,1,2,0:T(8,128)(2,1)S(1)} %get-tuple-element.81, f32[4,64,8]{2,1,0:T(8,128)S(1)} %copy.57), kind=kOutput, calls=%fused_computation.31 | convolution fusion | flops 268697600 | bytes 3678208 | tf_op jit(solution)/shard_map/grjn,ngd->grjd/dot_general | solution.py:64
  102.4 58.1 %all-gather.5.cloned.1.call-done = bf16[2048,1024]{1,0:T(8,128)(2,1)} async-done(((bf16[64,1024]{1,0:T(8,128)(2,1)}), bf16[2048,1024]{1,0:T(8,128)(2,1)}) %all-gather.5.cloned.1.call-update) | async-done | bytes 4194320 | tf_op jit(solution)/shard_map/all_gather | solution.py:94
  160.5 34.9 %conditional.1 = (f32[4,64,8]{2,1,0:T(8,128)S(1)}, f32[4,64,8,128]{3,2,1,0:T(8,128)}) conditional(s32[]{:T(128)} %convert_element_type.57, (f32[4,64,8]{1,2,0:T(8,128)S(1)}, f32[4,64,8,128]{3,2,1,0:T(8,128)}) %tuple.15, (s32[]{:T(128)}, s32[64,1]{0,1:T(1,128)S(1)}, s32[64,2048]{1,0:T(8,128)S(1)}, bf16[2048,1024]{1,0:T(8,128)(2,1)}, ...), branch_computations={%region_4.5_spmd, %region_5.8_spmd} | conditional | flops 2194280448 | bytes 75121424 | solution.py:97
  160.5 0.1 broadcast_compare_fusion
  160.7 6.6 %copy.64 = bf16[2048,1024]{0,1:T(8,128)(2,1)} copy(bf16[2048,1024]{1,0:T(8,128)(2,1)} %get-tuple-element.70) | data formatting | bytes 8388608 | tf_op jit(solution)/shard_map
  167.2 2.5 fusion.36
  169.8 7.8 %select_reduce_fusion = (f32[4,64,8]{2,1,0:T(8,128)S(1)}, f32[4,64,8,2048]{3,2,1,0:T(8,128)}) fusion(pred[64,2048]{1,0:T(8,128)(4,1)S(1)} %broadcast_compare_fusion, bf16[2048,4,128,1]{0,2,3,1:T(8,128)(2,1)S(1)} %bitcast.69, bf16[64,4,8,128]{3,2,1,0:T(8,128)(2,1)S(1)} %get-tuple-element.71), kind=kOutput, calls=%fused_computation.2 | convolution fusion | flops 1086322688 | bytes 19537920 | tf_op jit(solution)/shard_map/cond/branch_1_fun/rgjd,ngd->grjn/dot_general | solution.py:56
  177.6 0.1 copy.66
  177.7 8.3 %fusion.1 = f32[4,64,8]{2,1,0:T(8,128)S(1)} fusion(f32[4,64,8,2048]{3,2,1,0:T(8,128)} %get-tuple-element.80, f32[4,64,8]{2,1,0:T(8,128)S(1)} %max.2, pred[64,2048]{1,0:T(8,128)(4,1)S(1)} %broadcast_compare_fusion), kind=kLoop, calls=%fused_computation.4 | loop fusion | flops 16775168 | bytes 16924672 | tf_op jit(solution)/shard_map/cond/branch_1_fun/reduce_sum | solution.py:63
  186.0 0.1 copy.67
  186.1 9.3 %fusion.5 = f32[4,64,8,128]{3,2,1,0:T(8,128)} fusion(bf16[2048,4,128,1]{0,2,3,1:T(8,128)(2,1)S(1)} %bitcast.76, f32[4,64,8,2048]{3,2,1,0:T(8,128)} %get-tuple-element.80, f32[4,64,8]{2,1,0:T(8,128)S(1)} %max.2, pred[64,2048]{1,0:T(8,128)(4,1)S(1)} %broadcast_compare_fusion, f32[4,64,8,128]{3,2,1,0:T(8,128)} %get-tuple-element.32, ...), kind=kOutput, calls=%fused_computation.7 | convolution fusion | flops 1091043328 | bytes 21118976 | tf_op jit(solution)/shard_map/cond/branch_1_fun/grjn,ngd->grjd/dot_general | solution.py:64
  195.4 1.6 divide_bitcast_fusion
  197.0 0.1 copy.68
  197.1 0.2 reshape.140
  197.4 0.1 fusion.28
  197.5 3.4 %collective-permute-start = (bf16[1,64,4096]{2,1,0:T(8,128)(2,1)S(1)}, bf16[1,64,4096]{2,1,0:T(8,128)(2,1)S(1)}, u32[]{:S(2)}, u32[]{:S(2)}) collective-permute-start(bf16[1,64,4096]{2,1,0:T(8,128)(2,1)S(1)} %fusion.28), channel_id=1, source_target_pairs={{480,0},{0,32},{32,64},{64,96},{96,128},{128,160},{160,192},{192,2... | collective-permute-start | bytes 1572872 | tf_op jit(solution)/shard_map/ppermute | solution.py:15
  200.8 0.1 copy.62
  200.9 0.7 convert_element_type.67
  201.7 51.6 %collective-permute-done = bf16[1,64,4096]{2,1,0:T(8,128)(2,1)S(1)} collective-permute-done((bf16[1,64,4096]{2,1,0:T(8,128)(2,1)S(1)}, bf16[1,64,4096]{2,1,0:T(8,128)(2,1)S(1)}, u32[]{:S(2)}, u32[]{:S(2)}) %collective-permute-start) | collective-permute-done | bytes 524320 | tf_op jit(solution)/shard_map/ppermute | solution.py:15
  253.3 0.8 copy.108
  (23 shorter events, 0.2 us)
Async XLA Ops:
  7.2 5.7 %copy-start = (bf16[1,64,4096]{2,1,0:T(8,128)(2,1)S(1)}, bf16[1,64,4096]{2,1,0:T(8,128)(2,1)}, u32[]{:S(2)}) copy-start(bf16[1,64,4096]{2,1,0:T(8,128)(2,1)} %param.9) | copy-start | bytes 1572868
  7.2 5.4 %copy-start.3 = (bf16[1,4096]{1,0:T(2,128)(2,1)S(1)}, bf16[1,4096]{1,0:T(2,128)(2,1)}, u32[]{:S(2)}) copy-start(bf16[1,4096]{1,0:T(2,128)(2,1)} %param.10) | copy-start | bytes 24580
  7.2 5.5 %copy-start.4 = (s32[1,8]{1,0:T(1,128)S(1)}, s32[1,8]{1,0:T(1,128)}, u32[]{:S(2)}) copy-start(s32[1,8]{1,0:T(1,128)} %param.15) | copy-start | bytes 100
  7.2 76.3 %all-gather.3.cloned.1.call-start = ((), (), s32[]{:S(2)}) async-start(), calls=%async_computation | async-start | bytes 6488064 | tf_op jit(solution)/shard_map/all_gather | solution.py:79
  9.7 150.7 %all-gather.5.cloned.1.call-start = ((), (), s32[]{:S(2)}) async-start(), calls=%async_computation.1 | async-start | bytes 4325376 | tf_op jit(solution)/shard_map/all_gather | solution.py:94
  90.1 3.7 %copy-start.2 = (bf16[1,64,4096]{2,1,0:T(8,128)(2,1)S(1)}, bf16[1,64,4096]{2,1,0:T(8,128)(2,1)}, u32[]{:S(2)}) copy-start(bf16[1,64,4096]{2,1,0:T(8,128)(2,1)} %param.11) | copy-start | bytes 1572868
  195.4 2.0 copy-start.1
  197.5 55.8 %collective-permute-start = (bf16[1,64,4096]{2,1,0:T(8,128)(2,1)S(1)}, bf16[1,64,4096]{2,1,0:T(8,128)(2,1)S(1)}, u32[]{:S(2)}, u32[]{:S(2)}) collective-permute-start(bf16[1,64,4096]{2,1,0:T(8,128)(2,1)S(1)} %fusion.28), channel_id=1, source_target_pairs={{480,0},{0,32},{32,64},{64,96},{96,128},{128,160},{160,192},{192,2... | collective-permute-start | bytes 1572872 | tf_op jit(solution)/shard_map/ppermute | solution.py:15
Sparse Core Ops, SparseCore 0:
  10.7 72.7 all-gather.2
  93.9 66.5 all-gather.4
where the time goes:
time: 262 us; the launch traced here: 261 us
  waiting for transfers between devices  178 us (68%)
  matrix products  24.9 us (10%)
  local copies, waits for them, and re-layouts  21.7 us (8%)
  other arithmetic  18 us (7%)
  between operations  14.3 us (5%)
  starting transfers between devices  3.46 us (1%)
    all_gather x1, waiting for transfers between devices, local(): lax.all_gather(packed, 'zero', axis=0, tiled=True)  68.7 us
    all_gather x1, waiting for transfers between devices, local(): portion = lax.all_gather(kv_new, 'zero', axis=0, tiled=True)  58.1 us
    ppermute x1, waiting for transfers between devices, passed_along(): return lax.ppermute(block, axis, route)  51.6 us
    dot_general x2, matrix products, absorb(): jnp.einsum('grjn,ngd->grjd', weights.astype(jnp.bfloat16), value_grid, pr...  12.7 us
    dot_general x2, matrix products, absorb(): jnp.einsum('rgjd,ngd->grjn', query_grid, key_grid, preferred_element_type...  8.59 us
    reduce_sum x1, other arithmetic, absorb(): new_sum = run_sum * shrink + jnp.sum(weights, axis=-1)  8.27 us
    another operation x3, local copies, waits for them, and re-layouts  6.73 us
  transfers between devices with their start and end apart: 3, of which 3 were waited for; matrix products, arithmetic and copies ran while one was open for 5% of the time, Pallas kernels for 0%

commit v1 on v0

--- a/solution.py
+++ b/solution.py
@@ -76,9 +76,9 @@
     packed = jnp.concatenate(
         [panel_blocks[0].reshape(weight_rows, block_size), cache_local], axis=0
     )
-    gathered = lax.all_gather(packed, "zero", axis=0, tiled=True).reshape(
-        zero_size, packed.shape[0], block_size
-    )
+    gathered = jnp.concatenate(
+        lax.all_to_all(jnp.stack([packed] * lax.axis_size("zero")), "zero", 0, 0), axis=0
+    ).reshape(zero_size, packed.shape[0], block_size)
     all_blocks = gathered[:, :weight_rows].reshape(zero_size * local_slots, block_size, block_size)
     cache_portion = gathered[:, weight_rows:].reshape(
         zero_size * cached_kv.shape[1], cached_kv.shape[2]

time: 262 us -> 340 us (1.30)
  waiting for transfers between devices: 178 us -> 246 us
  starting transfers between devices: 3.46 us -> 12.8 us
    all_to_all x0 -> x1, waiting for transfers between devices: none -> 135 us  [local(): lax.all_to_all(jnp.stack([packed] * lax.axis_size('zero')), 'zero', 0, 0)]
    all_gather x1 -> x0, waiting for transfers between devices: 68.7 us -> none  [local(): lax.all_gather(packed, 'zero', axis=0, tiled=True)]
    all_to_all x0 -> x1, starting transfers between devices: none -> 9.33 us  [local(): lax.all_to_all(jnp.stack([packed] * lax.axis_size('zero')), 'zero', 0, 0)]
    another operation x3 -> x4, local copies, waits for them, and re-layouts: 6.73 us -> 10.8 us
  transfers between devices with their start and end apart: 3 -> 3, of which waited for: 3 -> 3; matrix products, arithmetic and copies ran while one was open for 5% -> 4% of each run, Pallas kernels for 0% -> 0%
where the time goes in v1:
time: 340 us; the launch traced here: 339 us
  waiting for transfers between devices  246 us (72%)
  matrix products  24.9 us (7%)
  local copies, waits for them, and re-layouts  24.4 us (7%)
  other arithmetic  16.3 us (5%)
  between operations  14.3 us (4%)
  starting transfers between devices  12.8 us (4%)
    all_to_all x1, waiting for transfers between devices, local(): lax.all_to_all(jnp.stack([packed] * lax.axis_size('zero')), 'zero', 0, 0)  135 us
    all_gather x1, waiting for transfers between devices, local(): portion = lax.all_gather(kv_new, 'zero', axis=0, tiled=True)  59.8 us
    ppermute x1, waiting for transfers between devices, passed_along(): return lax.ppermute(block, axis, route)  51.6 us
    dot_general x2, matrix products, absorb(): jnp.einsum('grjn,ngd->grjd', weights.astype(jnp.bfloat16), value_grid, pr...  12.7 us
    all_to_all x1, starting transfers between devices, local(): lax.all_to_all(jnp.stack([packed] * lax.axis_size('zero')), 'zero', 0, 0)  9.33 us
    dot_general x2, matrix products, absorb(): jnp.einsum('rgjd,ngd->grjn', query_grid, key_grid, preferred_element_type...  8.58 us
    reduce_sum x1, other arithmetic, absorb(): new_sum = run_sum * shrink + jnp.sum(weights, axis=-1)  8.27 us
  transfers between devices with their start and end apart: 3, of which 3 were waited for; matrix products, arithmetic and copies ran while one was open for 4% of the time, Pallas kernels for 0%

profile of v1, /device:TPU:96, one launch (start us, length us, event | category | flops | bytes accessed | tf_op | source)
XLA Modules:
  0.0 339.1 jit_solution(9160665678906860108)
XLA Ops:
  7.2 0.8 reshape_squeeze.15
  7.9 0.9 pad_maximum_fusion
  8.9 4.1 %stack.2 = bf16[32,768,128]{2,1,0:T(8,128)(2,1)} broadcast(bf16[768,128]{1,0:T(8,128)(2,1)S(1)} %pad_maximum_fusion), dimensions={1,2} | broadcast | bytes 6488064 | tf_op jit(solution)/shard_map/stack | solution.py:80
  13.0 9.3 %all-to-all-start = ((bf16[32,768,128]{2,1,0:T(8,128)(2,1)}), bf16[32,768,128]{2,1,0:T(8,128)(2,1)}, u32[]{:S(2)}, u32[]{:S(2)}) async-start(bf16[32,768,128]{2,1,0:T(8,128)(2,1)} %stack.2), calls=%async_computation | async-start | bytes 12582912 | tf_op jit(solution)/shard_map/all_to_all | solution.py:80
  22.3 0.0 all-gather.2.cloned.1.call-start
  22.4 0.1 reshape_squeeze.18
  22.4 0.1 reshape_squeeze.17
  22.5 0.1 convert_bitcast_fusion
  22.6 0.2 copy.84
  22.8 0.1 fusion.33
  22.9 0.1 reshape.141
  23.0 0.2 fusion.27
  23.2 0.7 fusion.30
  23.9 1.1 gather_fusion
  25.0 134.9 %all-to-all-done = bf16[32,768,128]{2,1,0:T(8,128)(2,1)} async-done(((bf16[32,768,128]{2,1,0:T(8,128)(2,1)}), bf16[32,768,128]{2,1,0:T(8,128)(2,1)}, u32[]{:S(2)}, u32[]{:S(2)}) %all-to-all-start) | async-done | bytes 6291488 | tf_op jit(solution)/shard_map/all_to_all | solution.py:80
  160.0 2.8 slice.29
  162.8 3.7 %broadcast_multiply_fusion = f32[160,128,64]{1,2,0:T(8,128)} fusion(f32[160]{0:T(256)S(1)} %reshape.141, bf16[160,128,128]{2,1,0:T(8,128)(2,1)S(1)} %bitcast.67, bf16[160,64,128]{2,1,0:T(8,128)(2,1)S(1)} %gather_fusion, pred[160]{0:T(512)(128)(4,1)S(1)} %compare_and_fusion), kind=kOutput, calls=%fused_computation.24 | convolution fusion | flops 338165760 | bytes 13108000 | tf_op jit(solution)/shard_map/rsk,skn->rsn/dot_general | solution.py:87
  166.5 3.0 reduce_sum.38
  169.5 0.7 copy_bitcast_fusion
  170.2 0.1 copy.83
  170.3 1.3 slice.26
  171.6 0.5 reshape.133
  172.1 0.1 fusion.37
  172.2 0.2 copy.54
  172.4 0.8 bitcast_reduce_fusion
  173.2 1.1 fusion.13
  174.3 0.1 copy.57
  174.4 1.0 copy.58
  175.4 3.4 %fusion.23 = f32[4,64,8,128]{3,2,1,0:T(8,128)} fusion(bf16[512,4,128,1]{0,2,3,1:T(8,128)(2,1)} %bitcast.75, bf16[4,64,8,512]{3,1,2,0:T(8,128)(2,1)S(1)} %get-tuple-element.81, f32[4,64,8]{2,1,0:T(8,128)S(1)} %copy.57), kind=kOutput, calls=%fused_computation.31 | convolution fusion | flops 268697600 | bytes 3678208 | tf_op jit(solution)/shard_map/grjn,ngd->grjd/dot_general | solution.py:64
  178.8 59.8 %all-gather.2.cloned.1.call-done = bf16[2048,1024]{1,0:T(8,128)(2,1)} async-done(((bf16[64,1024]{1,0:T(8,128)(2,1)}), bf16[2048,1024]{1,0:T(8,128)(2,1)}) %all-gather.2.cloned.1.call-update) | async-done | bytes 4194320 | tf_op jit(solution)/shard_map/all_gather | solution.py:94
  238.7 34.9 %conditional.1 = (f32[4,64,8]{2,1,0:T(8,128)S(1)}, f32[4,64,8,128]{3,2,1,0:T(8,128)}) conditional(s32[]{:T(128)} %convert_element_type.57, (f32[4,64,8]{1,2,0:T(8,128)S(1)}, f32[4,64,8,128]{3,2,1,0:T(8,128)}) %tuple.15, (s32[]{:T(128)}, s32[64,1]{0,1:T(1,128)S(1)}, s32[64,2048]{1,0:T(8,128)S(1)}, bf16[2048,1024]{1,0:T(8,128)(2,1)}, ...), branch_computations={%region_4.5_spmd, %region_5.8_spmd} | conditional | flops 2194280448 | bytes 75121424 | solution.py:97
  238.7 0.1 broadcast_compare_fusion
  238.9 6.6 %copy.64 = bf16[2048,1024]{0,1:T(8,128)(2,1)} copy(bf16[2048,1024]{1,0:T(8,128)(2,1)} %get-tuple-element.70) | data formatting | bytes 8388608 | tf_op jit(solution)/shard_map
  245.4 2.5 fusion.36
  248.0 7.8 %select_reduce_fusion = (f32[4,64,8]{2,1,0:T(8,128)S(1)}, f32[4,64,8,2048]{3,2,1,0:T(8,128)}) fusion(pred[64,2048]{1,0:T(8,128)(4,1)S(1)} %broadcast_compare_fusion, bf16[2048,4,128,1]{0,2,3,1:T(8,128)(2,1)S(1)} %bitcast.68, bf16[64,4,8,128]{3,2,1,0:T(8,128)(2,1)S(1)} %get-tuple-element.71), kind=kOutput, calls=%fused_computation.2 | convolution fusion | flops 1086322688 | bytes 19537920 | tf_op jit(solution)/shard_map/cond/branch_1_fun/rgjd,ngd->grjn/dot_general | solution.py:56
  255.8 0.1 copy.66
  255.9 8.3 %fusion.1 = f32[4,64,8]{2,1,0:T(8,128)S(1)} fusion(f32[4,64,8,2048]{3,2,1,0:T(8,128)} %get-tuple-element.80, f32[4,64,8]{2,1,0:T(8,128)S(1)} %max.2, pred[64,2048]{1,0:T(8,128)(4,1)S(1)} %broadcast_compare_fusion), kind=kLoop, calls=%fused_computation.4 | loop fusion | flops 16775168 | bytes 16924672 | tf_op jit(solution)/shard_map/cond/branch_1_fun/reduce_sum | solution.py:63
  264.2 0.1 copy.67
  264.3 9.3 %fusion.5 = f32[4,64,8,128]{3,2,1,0:T(8,128)} fusion(bf16[2048,4,128,1]{0,2,3,1:T(8,128)(2,1)S(1)} %bitcast.73, f32[4,64,8,2048]{3,2,1,0:T(8,128)} %get-tuple-element.80, f32[4,64,8]{2,1,0:T(8,128)S(1)} %max.2, pred[64,2048]{1,0:T(8,128)(4,1)S(1)} %broadcast_compare_fusion, f32[4,64,8,128]{3,2,1,0:T(8,128)} %get-tuple-element.32, ...), kind=kOutput, calls=%fused_computation.7 | convolution fusion | flops 1091043328 | bytes 21118976 | tf_op jit(solution)/shard_map/cond/branch_1_fun/grjn,ngd->grjd/dot_general | solution.py:64
  273.6 1.6 divide_bitcast_fusion
  275.2 0.1 copy.68
  275.3 0.2 reshape.138
  275.5 0.1 fusion.28
  275.6 3.4 collective-permute-start
  279.0 0.1 copy.62
  279.1 0.7 convert_element_type.67
  279.8 51.6 %collective-permute-done = bf16[1,64,4096]{2,1,0:T(8,128)(2,1)S(1)} collective-permute-done((bf16[1,64,4096]{2,1,0:T(8,128)(2,1)S(1)}, bf16[1,64,4096]{2,1,0:T(8,128)(2,1)S(1)}, u32[]{:S(2)}, u32[]{:S(2)}) %collective-permute-start) | collective-permute-done | bytes 524320 | tf_op jit(solution)/shard_map/ppermute | solution.py:15
  331.5 0.8 copy.108
  (25 shorter events, 0.2 us)
Async XLA Ops:
  12.9 9.4 %copy-start.3 = (s32[1,8,20]{2,1,0:T(8,128)S(1)}, s32[1,8,20]{2,1,0:T(8,128)}, u32[]{:S(2)}) copy-start(s32[1,8,20]{2,1,0:T(8,128)} %param.14) | copy-start | bytes 1924
  12.9 9.6 %copy-start = (bf16[1,64,4096]{2,1,0:T(8,128)(2,1)S(1)}, bf16[1,64,4096]{2,1,0:T(8,128)(2,1)}, u32[]{:S(2)}) copy-start(bf16[1,64,4096]{2,1,0:T(8,128)(2,1)} %param.9) | copy-start | bytes 1572868
  12.9 9.8 %copy-start.4 = (bf16[1,4096]{1,0:T(2,128)(2,1)S(1)}, bf16[1,4096]{1,0:T(2,128)(2,1)}, u32[]{:S(2)}) copy-start(bf16[1,4096]{1,0:T(2,128)(2,1)} %param.10) | copy-start | bytes 24580
  13.0 9.9 %copy-start.5 = (s32[1,8]{1,0:T(1,128)S(1)}, s32[1,8]{1,0:T(1,128)}, u32[]{:S(2)}) copy-start(s32[1,8]{1,0:T(1,128)} %param.15) | copy-start | bytes 100
  13.0 147.0 %all-to-all-start = ((bf16[32,768,128]{2,1,0:T(8,128)(2,1)}), bf16[32,768,128]{2,1,0:T(8,128)(2,1)}, u32[]{:S(2)}, u32[]{:S(2)}) async-start(bf16[32,768,128]{2,1,0:T(8,128)(2,1)} %stack.2), calls=%async_computation | async-start | bytes 12582912 | tf_op jit(solution)/shard_map/all_to_all | solution.py:80
  22.3 216.3 %all-gather.2.cloned.1.call-start = ((), (), s32[]{:S(2)}) async-start(), calls=%async_computation.1 | async-start | bytes 4325376 | tf_op jit(solution)/shard_map/all_gather | solution.py:94
  166.5 3.7 %copy-start.2 = (bf16[1,64,4096]{2,1,0:T(8,128)(2,1)S(1)}, bf16[1,64,4096]{2,1,0:T(8,128)(2,1)}, u32[]{:S(2)}) copy-start(bf16[1,64,4096]{2,1,0:T(8,128)(2,1)} %param.11) | copy-start | bytes 1572868
  273.6 2.0 copy-start.1
  275.6 55.8 %collective-permute-start = (bf16[1,64,4096]{2,1,0:T(8,128)(2,1)S(1)}, bf16[1,64,4096]{2,1,0:T(8,128)(2,1)S(1)}, u32[]{:S(2)}, u32[]{:S(2)}) collective-permute-start(bf16[1,64,4096]{2,1,0:T(8,128)(2,1)S(1)} %fusion.28), channel_id=1, source_target_pairs={{480,0},{0,32},{32,64},{64,96},{96,128},{128,160},{160,192},{192,2... | collective-permute-start | bytes 1572872 | tf_op jit(solution)/shard_map/ppermute | solution.py:15
Sparse Core Ops, SparseCore 0:
  170.3 68.2 all-gather.1
